TPU v7x, 128 devices: a whole 4x4x4 slice. The times are simulated.
128 devices in a mesh: seq: 16 (over y, x_lo, core), tp: 8 (over z, x_hi).
Axes of the slice: x: 4 (x_hi: 2, x_lo: 2; x = x_hi * 2 + x_lo), y: 4, z: 4, core: 2. Of those that a mesh axis runs over, the one named last changes fastest.
Arguments:
- tokens: bfloat16 [8192, 4096], P('seq'), may hold values from -6 to 6
- norm_gain: bfloat16 [4096], replicated, may hold values from 0.099609375 to 1.8984375
- w_query: bfloat16 [4096, 4096], P(None, 'tp'), may hold values from -4 to 4
- w_key: bfloat16 [4096, 512], replicated, may hold values from -1 to 1
- w_value: bfloat16 [4096, 512], replicated, may hold values from -0.09375 to 0.09375
- w_out: bfloat16 [4096, 4096], P('tp'), may hold values from -0.375 to 0.375
- prompt_lengths: int32 [16], replicated, may hold values from 1 to 6144, 8192 in all
- page_slots: int32 [64], replicated, may hold values from 0 to 63, each once
Outputs:
- attended: bfloat16 [8192, 4096], P(('seq', 'tp'))
- kv_cache: bfloat16 [64, 128, 1024], P('seq', None, 'tp')
Inputs may be any that keep to these rules, and one draw needn't show every extreme that they name: `prompt_lengths`: the lengths sum to 8192; the longest prompt has exactly 6144 tokens. `page_slots`: every value appears exactly once.
All inputs are finite; a program needn't handle non-finite values.
Results may differ from a plain program's by a relative error of at most 0.015.
Values may be sent and summed in bfloat16 or wider, within the bound.
No kernel may reach another device: no remote copies, remote signals or barrier semaphores. Data moves between devices by JAX's collectives and lax.ppermute only.
A program may use at most 128 MiB of HBM per device.

v0:
```python
import jax
import jax.numpy as jnp
from jax import lax
from jax.sharding import PartitionSpec as P

HD = 128
PAGE = 128
epsilon = 1e-05
rope_base = 5000000.0


def segment_info(token_index, prompt_lengths):
    prompt_ends = jnp.cumsum(prompt_lengths)
    finished = prompt_ends[None, :] <= token_index[:, None]
    segment = jnp.sum(finished.astype(jnp.int32), axis=1)
    offset = jnp.sum(jnp.where(finished, prompt_lengths[None, :], 0), axis=1)
    return (segment, token_index - offset)


def rotate(vectors, position):
    half_size = HD // 2
    frequency = rope_base ** (-(2.0 * jnp.arange(half_size, dtype=jnp.float32)) / HD)
    angle = position.astype(jnp.float32)[:, None] * frequency[None, :]
    cosine = jnp.cos(angle)[:, None, :]
    sine = jnp.sin(angle)[:, None, :]
    first_half = vectors[..., :half_size]
    second_half = vectors[..., half_size:]
    return jnp.concatenate(
        [first_half * cosine - second_half * sine, second_half * cosine + first_half * sine],
        axis=-1,
    )


def normalize(tokens, norm_gain):
    hidden = tokens.astype(jnp.float32)
    factor = lax.rsqrt(jnp.mean(hidden * hidden, axis=-1, keepdims=True) + epsilon)
    return (hidden * factor * norm_gain.astype(jnp.float32)).astype(jnp.bfloat16)


def attend(
    head_state,
    group_queries,
    group_index,
    group_segment,
    key_rows,
    value_rows,
    key_index,
    key_segment,
):
    running_max, running_sum, weighted = head_state
    scores = jnp.einsum(
        "rhd,nd->hrn", group_queries, key_rows, preferred_element_type=jnp.float32
    ) * HD ** (-0.5)
    visible = (
        (key_index[None, :] <= group_index[:, None])
        & (key_segment[None, :] == group_segment[:, None])
    )[None]
    fresh_max = jnp.maximum(running_max, jnp.max(jnp.where(visible, scores, -1e30), axis=2))
    weights = jnp.where(visible, jnp.exp(scores - fresh_max[..., None]), 0.0)
    shrink = jnp.exp(running_max - fresh_max)
    running_sum = running_sum * shrink + jnp.sum(weights, axis=2)
    weighted = weighted * shrink[..., None] + jnp.einsum(
        "hrn,nd->hrd", weights.astype(jnp.bfloat16), value_rows, preferred_element_type=jnp.float32
    )
    return (fresh_max, running_sum, weighted)


def on_device(tokens, norm_gain, w_query, w_key, w_value, w_out, prompt_lengths, page_slots):
    row_count = tokens.shape[0]
    tp_count = lax.axis_size("tp")
    seq_rank = lax.axis_index("seq")
    tp_rank = lax.axis_index("tp")
    heads_here = w_query.shape[1] // HD
    kv_heads = w_key.shape[1] // HD
    sharing = tp_count // kv_heads
    kv_head = tp_rank // sharing
    token_index = seq_rank * row_count + jnp.arange(row_count, dtype=jnp.int32)
    segment, position = segment_info(token_index, prompt_lengths)
    normed = normalize(tokens, norm_gain)
    queries = rotate(
        jnp.dot(normed, w_query, preferred_element_type=jnp.float32).reshape(
            row_count, heads_here, HD
        ),
        position,
    ).astype(jnp.bfloat16)
    key_columns = lax.dynamic_slice_in_dim(w_key, kv_head * HD, HD, 1)
    value_columns = lax.dynamic_slice_in_dim(w_value, kv_head * HD, HD, 1)
    keys_here = rotate(
        jnp.dot(normed, key_columns, preferred_element_type=jnp.float32)[:, None, :], position
    )[:, 0].astype(jnp.bfloat16)
    values_here = jnp.dot(normed, value_columns, preferred_element_type=jnp.float32).astype(
        jnp.bfloat16
    )
    keys_values = jnp.concatenate([keys_here, values_here], axis=1)
    cache_width = 2 * HD // sharing
    cache_column = tp_rank % sharing * cache_width
    slots_here = row_count // PAGE
    cache_rows = jnp.arange(slots_here * PAGE, dtype=jnp.int32)
    page_total = page_slots.shape[0]
    groups = ((queries, token_index, segment),)

    def step_block(carried, block_input):
        states, cache_here = carried
        block_values, block_start = block_input
        block_size = block_values.shape[0]
        key_index = block_start + jnp.arange(block_size, dtype=jnp.int32)
        key_segment, unused_key_position = segment_info(key_index, prompt_lengths)
        key_rows = block_values[:, :HD]
        value_rows = block_values[:, HD:]
        updated = []
        for head_state, group in zip(states, groups):
            group_queries, group_index, group_segment = group
            head_state = attend(
                head_state,
                group_queries,
                group_index,
                group_segment,
                key_rows,
                value_rows,
                key_index,
                key_segment,
            )
            updated.append(head_state)
        page_number = key_index // PAGE
        global_slot = jnp.sum(
            jnp.where(
                page_number[:, None] == jnp.arange(page_total, dtype=jnp.int32)[None, :],
                page_slots[None, :],
                0,
            ),
            axis=1,
        )
        cache_target = jnp.where(
            global_slot // slots_here == seq_rank,
            global_slot % slots_here * PAGE + key_index % PAGE,
            -1,
        )
        selector = (cache_rows[:, None] == cache_target[None, :]).astype(jnp.bfloat16)
        page_part = lax.dynamic_slice_in_dim(block_values, cache_column, cache_width, 1)
        cache_here = cache_here + jnp.dot(
            selector, page_part, preferred_element_type=jnp.float32
        ).astype(jnp.bfloat16)
        return ((tuple(updated), cache_here), None)

    initial_states = tuple(
        (
            (
                jnp.full((heads_here, group[1].shape[0]), -1e30, jnp.float32),
                jnp.zeros((heads_here, group[1].shape[0]), jnp.float32),
                jnp.zeros((heads_here, group[1].shape[0], HD), jnp.float32),
            )
            for group in groups
        )
    )
    initial_cache = jnp.zeros((slots_here * PAGE, cache_width), jnp.bfloat16)
    carried = (initial_states, initial_cache)
    shard_piece = lax.all_gather(keys_values, "seq", axis=0, tiled=True)
    piece_rows = shard_piece.shape[0]
    block_rows = 512
    blocks = shard_piece.reshape(piece_rows // block_rows, block_rows, 2 * HD)
    block_starts = block_rows * jnp.arange(piece_rows // block_rows, dtype=jnp.int32)
    carried, unused_output = lax.scan(step_block, carried, (blocks, block_starts))
    states, cache_here = carried
    outputs = [
        (weighted / running_sum[..., None])
        .transpose(1, 0, 2)
        .reshape(-1, heads_here * HD)
        .astype(jnp.bfloat16)
        for running_max, running_sum, weighted in states
    ]
    heads_out = outputs[0]
    attended = lax.psum_scatter(
        jnp.dot(heads_out, w_out, preferred_element_type=jnp.float32).astype(jnp.bfloat16),
        "tp",
        scatter_dimension=0,
        tiled=True,
    )
    return (attended, cache_here.reshape(slots_here, PAGE, cache_width))


def solution(mesh):
    placed = (P("seq", None), P(), P(None, "tp"), P(), P(), P("tp", None), P(), P())
    return jax.shard_map(
        on_device,
        mesh=mesh,
        in_specs=placed,
        out_specs=(P(("seq", "tp"), None), P("seq", None, "tp")),
        check_vma=False,
    )
```

profile of v0, /device:TPU:0, one launch (start us, length us, event | category | flops | bytes accessed | tf_op | source)
XLA Modules:
  0.0 305.7 jit_solution(4409422071376044708)
XLA Ops:
  8.1 3.1 %fusion.33 = f32[512]{0:T(512)S(1)} fusion(bf16[512,4096]{1,0:T(8,128)(2,1)} %param.10), kind=kLoop, calls=%fused_computation.59 | loop fusion | flops 6290944 | bytes 4196352 | tf_op jit(solution)/shard_map/reduce_sum | solution.py:36
  11.4 4.2 %convolution_convert_fusion.2 = bf16[512,128]{0,1:T(8,128)(2,1)S(1)} fusion(bf16[4096,512]{1,0:T(8,128)(2,1)} %param.14, s32[]{:T(128)S(6)} %select_n.116, bf16[512,4096]{1,0:T(8,128)(2,1)} %param.10, f32[4096]{0:T(1024)S(1)} %convert_element_type.64, f32[512]{0:T(512)S(1)} %add_rsqrt_fusion), kind=kOutput, calls=%fused_computation.64 | convolution fusion | flops 545325056 | bytes 5392388 | tf_op jit(solution)/shard_map/dot_general | solution.py:91
  15.6 2.8 convolution_bitcast_fusion
  20.1 5.9 %fusion.50 = f32[512,512]{0,1:T(8,128)S(1)} fusion(bf16[4096,512]{1,0:T(8,128)(2,1)} %param.12, bf16[512,4096]{1,0:T(8,128)(2,1)} %param.10, f32[4096]{0:T(1024)S(1)} %convert_element_type.64, f32[512]{0:T(512)S(1)} %add_rsqrt_fusion), kind=kOutput, calls=%fused_computation.96 | convolution fusion | flops 2155872256 | bytes 9455616 | tf_op jit(solution)/shard_map/dot_general | solution.py:81
  28.5 31.4 %all-gather.2.cloned.1.call-done = bf16[8192,256]{0,1:T(8,128)(2,1)} async-done(((bf16[512,256]{0,1:T(8,128)(2,1)}), bf16[8192,256]{0,1:T(8,128)(2,1)}) %all-gather.2.cloned.1.call-update) | async-done | bytes 4194320 | tf_op jit(solution)/shard_map/all_gather | solution.py:157
  59.8 6.4 %copy.25 = bf16[8192,256]{1,0:T(8,128)(2,1)} copy(bf16[8192,256]{0,1:T(8,128)(2,1)} %all-gather.2.cloned.1.call-done) | data formatting | bytes 8388608
  66.2 141.5 %while.20 = (s32[]{:T(128)}, f32[4,512]{1,0:T(4,128)S(1)}, f32[4,512]{1,0:T(4,128)S(1)}, f32[4,512,128]{2,1,0:T(8,128)S(1)}, bf16[512,128]{1,0:T(8,128)(2,1)S(1)...) while((s32[]{:T(128)}, f32[4,512]{1,0:T(4,128)S(1)}, ...), condition=%wide.region_9.10_spmd.clone, body=%wide.region_4.9_spmd.clone.sunk | while | flops 617704960 | bytes 17593384 | solution.py:162
  73.5 1.5 fusion.75
  77.8 1.4 fusion.76
  82.3 1.5 fusion.75
  86.7 1.4 fusion.76
  91.2 1.5 fusion.75
  95.5 1.4 fusion.76
  100.0 1.5 fusion.75
  104.3 1.4 fusion.76
  108.9 1.5 fusion.75
  113.2 1.4 fusion.76
  117.7 1.5 fusion.75
  126.6 1.5 fusion.75
  130.9 1.4 fusion.76
  135.4 1.5 fusion.75
  144.3 1.5 fusion.75
  153.1 1.5 fusion.75
  162.0 1.5 fusion.75
  170.8 1.5 fusion.75
  179.6 1.5 fusion.75
  188.5 1.5 fusion.75
  192.8 1.4 fusion.76
  197.3 1.5 fusion.75
  206.2 1.5 fusion.75
  208.2 6.5 %convolution_convert_fusion.1 = bf16[512,4096]{1,0:T(8,128)(2,1)} fusion(bf16[512,512]{0,1:T(8,128)(2,1)S(1)} %bitcast.68, bf16[512,4096]{1,0:T(8,128)(2,1)} %param.15), kind=kOutput, calls=%fused_computation.62 | convolution fusion | flops 2149580800 | bytes 8912896 | tf_op jit(solution)/shard_map/dot_general | solution.py:173
  214.7 84.1 %reduce-scatter.2.cloned.1.call-done = bf16[64,4096]{1,0:T(8,128)(2,1)} async-done(((bf16[512,4096]{1,0:T(8,128)(2,1)}), bf16[64,4096]{1,0:T(8,128)(2,1)}) %reduce-scatter.2.cloned.1.call-update) | async-done | bytes 524304 | tf_op jit(solution)/shard_map/reduce_scatter | solution.py:172
  (256 shorter events, 111.1 us)
Async XLA Ops:
  7.2 4.1 %copy-start.4 = (s32[16]{0:T(128)S(1)}, s32[16]{0:T(128)}, u32[]{:S(2)}) copy-start(s32[16]{0:T(128)} %param.16) | copy-start | bytes 196
  7.2 4.2 %copy-start.3 = (bf16[4096]{0:T(1024)(128)(2,1)S(1)}, bf16[4096]{0:T(1024)(128)(2,1)}, u32[]{:S(2)}) copy-start(bf16[4096]{0:T(1024)(128)(2,1)} %param.11) | copy-start | bytes 24580
  7.2 52.6 %all-gather.2.cloned.1.call-start = ((), (), s32[]{:S(2)}) async-start(), calls=%async_computation.1 | async-start | bytes 4456448 | tf_op jit(solution)/shard_map/all_gather | solution.py:157
  11.4 4.3 %copy-start = (bf16[512,4096]{1,0:T(8,128)(2,1)S(1)}, bf16[512,4096]{1,0:T(8,128)(2,1)}, u32[]{:S(2)}) copy-start(bf16[512,4096]{1,0:T(8,128)(2,1)} %param.10) | copy-start | bytes 12582916
  19.8 279.0 %reduce-scatter.2.cloned.1.call-start = ((), (), s32[]{:S(2)}) async-start(), calls=%async_computation.2 | async-start | bytes 4718592 | tf_op jit(solution)/shard_map/reduce_scatter | solution.py:172
  28.4 37.8 %copy-start.1 = (f32[4,512,128]{2,1,0:T(8,128)S(1)}, f32[4,512,128]{2,1,0:T(8,128)}, u32[]{:S(2)}) copy-start(f32[4,512,128]{2,1,0:T(8,128)} %custom-call.2) | copy-start | bytes 3145732
  28.5 37.8 %copy-start.2 = (s32[64]{0:T(128)S(1)}, s32[64]{0:T(128)}, u32[]{:S(2)}) copy-start(s32[64]{0:T(128)} %param.17) | copy-start | bytes 772
  207.7 7.0 %copy-start.5 = (bf16[512,128]{1,0:T(8,128)(2,1)}, bf16[512,128]{1,0:T(8,128)(2,1)S(1)}, u32[]{:S(2)}) copy-start(bf16[512,128]{1,0:T(8,128)(2,1)S(1)} %get-tuple-element.271) | copy-start | bytes 393220
Sparse Core Ops, SparseCore 0:
  19.9 39.8 all-gather.1
  214.9 83.9 reduce-scatter.1
where the time goes:
time: 308 us; the launch traced here: 306 us
  waiting for transfers between devices  115 us (37%)
  matrix products  81 us (26%)
  other arithmetic  60.7 us (20%)
  local copies, waits for them, and re-layouts  32.6 us (11%)
  between operations  14.3 us (5%)
    reduce_scatter x1, waiting for transfers between devices, on_device(): lax.psum_scatter(jnp.dot(heads_out, w_out, preferred_element_type=jnp.flo...  84.1 us
    all_gather x1, waiting for transfers between devices, on_device(): shard_piece = lax.all_gather(keys_values, 'seq', axis=0, tiled=True)  31.4 us
    dot_general x16, matrix products, attend(): jnp.einsum('hrn,nd->hrd', weights.astype(jnp.bfloat16), value_rows, prefe...  24.5 us
    dot_general x16, matrix products, step_block(): jnp.dot(selector, page_part, preferred_element_type=jnp.float32)  22.8 us
    squeeze x16, local copies, waits for them, and re-layouts, on_device(): lax.scan(step_block, carried, (blocks, block_starts))  15.6 us
    reduce_sum x16, other arithmetic, attend(): running_sum = running_sum * shrink + jnp.sum(weights, axis=2)  14.5 us
    dot_general x16, matrix products, attend(): jnp.einsum('rhd,nd->hrn', group_queries, key_rows, preferred_element_type...  14.2 us
    select_n x16, other arithmetic, step_block(): jnp.where(global_slot // slots_here == seq_rank, global_slot % slots_here...  10.5 us
  transfers between devices with their start and end apart: 2, of which 2 were waited for; matrix products, arithmetic and copies ran while one was open for 3% of the time, Pallas kernels for 0%

commit v1 on v0

--- a/solution.py
+++ b/solution.py
@@ -154,7 +154,8 @@
     )
     initial_cache = jnp.zeros((slots_here * PAGE, cache_width), jnp.bfloat16)
     carried = (initial_states, initial_cache)
-    shard_piece = lax.all_gather(keys_values, "seq", axis=0, tiled=True)
+    outgoing = jnp.stack([keys_values] * lax.axis_size("seq"))
+    shard_piece = jnp.concatenate(lax.all_to_all(outgoing, "seq", 0, 0), axis=0)
     piece_rows = shard_piece.shape[0]
     block_rows = 512
     blocks = shard_piece.reshape(piece_rows // block_rows, block_rows, 2 * HD)

time: 308 us -> 318 us (1.032)
  waiting for transfers between devices: 115 us -> 126 us
  starting transfers between devices: 0.26 us -> 5.86 us
  local copies, waits for them, and re-layouts: 32.6 us -> 28.8 us
    all_to_all x0 -> x1, waiting for transfers between devices: none -> 41.8 us  [on_device(): shard_piece = jnp.concatenate(lax.all_to_all(outgoing, 'seq', 0, 0), axis=0)]
    all_gather x1 -> x0, waiting for transfers between devices: 31.4 us -> none  [on_device(): shard_piece = lax.all_gather(keys_values, 'seq', axis=0, tiled=True)]
    unnamed x15 -> x14, local copies, waits for them, and re-layouts: 7.11 us -> 0.7 us
    all_to_all x0 -> x1, starting transfers between devices: none -> 5.64 us  [on_device(): shard_piece = jnp.concatenate(lax.all_to_all(outgoing, 'seq', 0, 0), axis=0)]
where the time goes in v1:
time: 318 us; the launch traced here: 316 us
  waiting for transfers between devices  126 us (40%)
  matrix products  81.1 us (26%)
  other arithmetic  58.7 us (18%)
  local copies, waits for them, and re-layouts  28.8 us (9%)
  between operations  14.3 us (4%)
  starting transfers between devices  5.86 us (2%)
    reduce_scatter x1, waiting for transfers between devices, on_device(): lax.psum_scatter(jnp.dot(heads_out, w_out, preferred_element_type=jnp.flo...  84.5 us
    all_to_all x1, waiting for transfers between devices, on_device(): shard_piece = jnp.concatenate(lax.all_to_all(outgoing, 'seq', 0, 0), axis=0)  41.8 us
    dot_general x16, matrix products, attend(): jnp.einsum('hrn,nd->hrd', weights.astype(jnp.bfloat16), value_rows, prefe...  24.5 us
    dot_general x16, matrix products, step_block(): jnp.dot(selector, page_part, preferred_element_type=jnp.float32)  22.8 us
    squeeze x16, local copies, waits for them, and re-layouts, on_device(): lax.scan(step_block, carried, (blocks, block_starts))  15.6 us
    reduce_sum x16, other arithmetic, attend(): running_sum = running_sum * shrink + jnp.sum(weights, axis=2)  14.5 us
    dot_general x16, matrix products, attend(): jnp.einsum('rhd,nd->hrn', group_queries, key_rows, preferred_element_type...  14.3 us
    select_n x16, other arithmetic, step_block(): jnp.where(global_slot // slots_here == seq_rank, global_slot % slots_here...  10 us
  transfers between devices with their start and end apart: 2, of which 2 were waited for; matrix products, arithmetic and copies ran while one was open for 3% of the time, Pallas kernels for 0%

profile of v1, /device:TPU:0, one launch (start us, length us, event | category | flops | bytes accessed | tf_op | source)
XLA Modules:
  0.0 316.4 jit_solution(9558670382999147603)
XLA Ops:
  8.1 3.1 fusion.33
  11.3 4.2 %convolution_convert_fusion.2 = bf16[512,128]{0,1:T(8,128)(2,1)S(1)} fusion(bf16[4096,512]{1,0:T(8,128)(2,1)} %param.14, s32[]{:T(128)S(6)} %select_n.116, bf16[512,4096]{1,0:T(8,128)(2,1)} %param.10, f32[4096]{0:T(1024)S(1)} %convert_element_type.64, f32[512]{0:T(512)S(1)} %add_rsqrt_fusion), kind=kOutput, calls=%fused_computation.64 | convolution fusion | flops 545325056 | bytes 5392388 | tf_op jit(solution)/shard_map/dot_general | solution.py:91
  15.6 2.8 convolution_bitcast_fusion
  19.2 2.4 stack.2
  21.6 5.6 %all-to-all-start = ((bf16[16,512,256]{2,1,0:T(8,128)(2,1)}), bf16[16,512,256]{2,1,0:T(8,128)(2,1)}, u32[]{:S(2)}, u32[]{:S(2)}) async-start(bf16[16,512,256]{2,1,0:T(8,128)(2,1)} %stack.2), calls=%async_computation | async-start | bytes 8388608 | tf_op jit(solution)/shard_map/all_to_all | solution.py:158
  27.5 5.9 %fusion.50 = f32[512,512]{0,1:T(8,128)S(1)} fusion(bf16[4096,512]{1,0:T(8,128)(2,1)} %param.12, bf16[512,4096]{1,0:T(8,128)(2,1)} %param.10, f32[4096]{0:T(1024)S(1)} %convert_element_type.64, f32[512]{0:T(512)S(1)} %add_rsqrt_fusion), kind=kOutput, calls=%fused_computation.96 | convolution fusion | flops 2155872256 | bytes 9455616 | tf_op jit(solution)/shard_map/dot_general | solution.py:81
  35.8 41.8 %all-to-all-done = bf16[16,512,256]{2,1,0:T(8,128)(2,1)} async-done(((bf16[16,512,256]{2,1,0:T(8,128)(2,1)}), bf16[16,512,256]{2,1,0:T(8,128)(2,1)}, u32[]{:S(2)}, u32[]{:S(2)}) %all-to-all-start) | async-done | bytes 4194336 | tf_op jit(solution)/shard_map/all_to_all | solution.py:158
  77.6 140.4 %while.20 = (s32[]{:T(128)}, f32[4,512]{1,0:T(4,128)S(1)}, f32[4,512]{1,0:T(4,128)S(1)}, f32[4,512,128]{2,1,0:T(8,128)S(1)}, bf16[512,128]{1,0:T(8,128)(2,1)S(1)...) while((s32[]{:T(128)}, f32[4,512]{1,0:T(4,128)S(1)}, ...), condition=%wide.region_9.10_spmd.clone, body=%wide.region_4.9_spmd.clone.sunk | while | flops 617704960 | bytes 17593384 | solution.py:163
  84.8 1.5 fusion.75
  93.6 1.5 fusion.75
  97.9 1.4 fusion.76
  102.4 1.5 fusion.75
  111.2 1.5 fusion.75
  115.4 1.4 fusion.76
  120.0 1.5 fusion.75
  128.7 1.5 fusion.75
  133.0 1.4 fusion.76
  137.5 1.5 fusion.75
  146.3 1.5 fusion.75
  150.5 1.4 fusion.76
  155.1 1.5 fusion.75
  163.8 1.5 fusion.75
  168.1 1.4 fusion.76
  172.6 1.5 fusion.75
  181.4 1.5 fusion.75
  185.6 1.4 fusion.76
  190.2 1.5 fusion.75
  199.0 1.5 fusion.75
  207.7 1.5 fusion.75
  216.5 1.5 fusion.75
  218.6 6.5 %convolution_convert_fusion.1 = bf16[512,4096]{1,0:T(8,128)(2,1)} fusion(bf16[512,512]{0,1:T(8,128)(2,1)S(1)} %bitcast.66, bf16[512,4096]{1,0:T(8,128)(2,1)} %param.15), kind=kOutput, calls=%fused_computation.62 | convolution fusion | flops 2149580800 | bytes 8912896 | tf_op jit(solution)/shard_map/dot_general | solution.py:174
  225.1 84.5 %reduce-scatter.2.cloned.1.call-done = bf16[64,4096]{1,0:T(8,128)(2,1)} async-done(((bf16[512,4096]{1,0:T(8,128)(2,1)}), bf16[64,4096]{1,0:T(8,128)(2,1)}) %reduce-scatter.2.cloned.1.call-update) | async-done | bytes 524304 | tf_op jit(solution)/shard_map/reduce_scatter | solution.py:173
  (256 shorter events, 110.8 us)
Async XLA Ops:
  7.2 4.0 %copy-start.4 = (s32[16]{0:T(128)S(1)}, s32[16]{0:T(128)}, u32[]{:S(2)}) copy-start(s32[16]{0:T(128)} %param.16) | copy-start | bytes 196
  7.2 4.1 %copy-start.3 = (bf16[4096]{0:T(1024)(128)(2,1)S(1)}, bf16[4096]{0:T(1024)(128)(2,1)}, u32[]{:S(2)}) copy-start(bf16[4096]{0:T(1024)(128)(2,1)} %param.11) | copy-start | bytes 24580
  11.3 4.3 %copy-start = (bf16[512,4096]{1,0:T(8,128)(2,1)S(1)}, bf16[512,4096]{1,0:T(8,128)(2,1)}, u32[]{:S(2)}) copy-start(bf16[512,4096]{1,0:T(8,128)(2,1)} %param.10) | copy-start | bytes 12582916
  21.6 56.0 %all-to-all-start = ((bf16[16,512,256]{2,1,0:T(8,128)(2,1)}), bf16[16,512,256]{2,1,0:T(8,128)(2,1)}, u32[]{:S(2)}, u32[]{:S(2)}) async-start(bf16[16,512,256]{2,1,0:T(8,128)(2,1)} %stack.2), calls=%async_computation | async-start | bytes 8388608 | tf_op jit(solution)/shard_map/all_to_all | solution.py:158
  27.2 282.4 %reduce-scatter.2.cloned.1.call-start = ((), (), s32[]{:S(2)}) async-start(), calls=%async_computation.2 | async-start | bytes 4718592 | tf_op jit(solution)/shard_map/reduce_scatter | solution.py:173
  33.6 44.1 %copy-start.2 = (s32[64]{0:T(128)S(1)}, s32[64]{0:T(128)}, u32[]{:S(2)}) copy-start(s32[64]{0:T(128)} %param.17) | copy-start | bytes 772
  34.3 43.4 %copy-start.1 = (f32[4,512,128]{2,1,0:T(8,128)S(1)}, f32[4,512,128]{2,1,0:T(8,128)}, u32[]{:S(2)}) copy-start(f32[4,512,128]{2,1,0:T(8,128)} %custom-call.2) | copy-start | bytes 3145732
  218.1 7.0 %copy-start.5 = (bf16[512,128]{1,0:T(8,128)(2,1)}, bf16[512,128]{1,0:T(8,128)(2,1)S(1)}, u32[]{:S(2)}) copy-start(bf16[512,128]{1,0:T(8,128)(2,1)S(1)} %get-tuple-element.271) | copy-start | bytes 393220
Sparse Core Ops, SparseCore 0:
  225.2 84.3 reduce-scatter.1
